TPU v7x, 32 devices: a whole 2x2x4 slice. The times are simulated.
32 devices in a mesh: gx: 8 (over y, x, core), gy: 4 (over z).
Axes of the slice: x: 2, y: 2, z: 4, core: 2. Of those that a mesh axis runs over, the one named last changes fastest.
Arguments:
- temp_start: float32 [8, 1024, 2048], P(None, ('gx', 'gy')), may hold values from -6 to 6
- heat_input: float32 [8, 1024, 2048], P(None, ('gx', 'gy')), may hold values from -3 to 3
- lateral: float32 [8], replicated, may hold values from 0.03 to 0.15
- vertical: float32 [7], replicated, may hold values from 0.03 to 0.15
- weighting: float32 [8], replicated, may hold values from -1 to 1
- modulus: float32 [1024, 2048], P('gx', 'gy'), may hold values from 0.3 to 3
- warp_prev: float32 [1024, 2048], P('gx', 'gy'), may hold values from -6 to 6
- joint_cell: int32 [65536], P(('gx', 'gy')), may hold values from 0 to 65535
- joint_owner: int32 [65536, 1], P(('gx', 'gy')), may hold values from 0 to 31; in each aligned block of 2048 rows (0 to 2047, 2048 to 4095, ...) at most 192 rows name the same one
- joint_strain: float32 [2, 32, 6144], P(None, ('gx', 'gy')), may hold values from -4 to 4
- joint_resist: float32 [32, 6144], P(('gx', 'gy')), may hold values from 1 to 2
Outputs:
- warpage: float32 [1024, 2048], P('gx', 'gy')
- strain_next: float32 [2, 32, 6144], P(None, ('gx', 'gy'))
- resist_next: float32 [32, 6144], P(('gx', 'gy'))
Inputs may be any that keep to these rules, and one draw needn't show every extreme that they name: `joint_owner`: among the 2048 joints of one device at most 192 have the same owner, and on some device exactly 192 do.
All inputs are finite; a program needn't handle non-finite values.
Results may differ from a plain program's by a relative error of at most 0.0003.
Values sent between devices are 32-bit elements; how exact they have to be, the bound alone decides.
No kernel may reach another device: no remote copies, remote signals or barrier semaphores. Data moves between devices by JAX's collectives and lax.ppermute only.
A program may use at most 320 MiB of HBM per device.

v0:
```python
import jax
import jax.numpy as jnp
from jax import lax
from jax.sharding import PartitionSpec as P

STEPS = 2
SWEEPS = 3
stiffness = 0.2
shear_mod = 0.6
rate_scale = 0.5
sat_level = 2.5
sat_power = 0.3
harden = 2.0


def with_halo(array, sides, width):
    for axis, dim in sides:
        count, length = (lax.axis_size(axis), array.shape[dim])
        up = [(i, (i + 1) % count) for i in range(count - 1)]
        down = [(j, i) for i, j in up]
        last = lax.slice_in_dim(array, length - width, length, axis=dim)
        leading = lax.slice_in_dim(array, 0, width, axis=dim)
        before = lax.ppermute(last, axis, up)
        after = lax.ppermute(leading, axis, down)
        array = jnp.concatenate([before, array, after], axis=dim)
    return array


def thermal_step(ext, heat_rows, lateral, vertical):
    cols = jnp.pad(ext, ((0, 0), (0, 0), (1, 1)))
    center = ext[:, 1:-1]
    lap = ext[:, 2:] + ext[:, :-2] + cols[:, 1:-1, 2:] + cols[:, 1:-1, :-2] - 4.0 * center
    flux = vertical[:, None, None] * (center[1:] - center[:-1])
    vert = jnp.pad(flux, ((0, 1), (0, 0), (0, 0))) - jnp.pad(flux, ((1, 0), (0, 0), (0, 0)))
    return center + lateral[:, None, None] * lap + vert + heat_rows


def moment_of(field, weighting):
    total = weighting[0] * field[0]
    for layer in range(1, field.shape[0]):
        total = total + weighting[layer] * field[layer]
    return total


def sweep(w_pad, e_pad, load):
    center = e_pad[1:-1, 1:-1]
    e_up = 0.5 * (center + e_pad[:-2, 1:-1])
    e_down = 0.5 * (center + e_pad[2:, 1:-1])
    e_left = 0.5 * (center + e_pad[1:-1, :-2])
    e_right = 0.5 * (center + e_pad[1:-1, 2:])
    numer = (
        load
        + e_up * w_pad[:-2, 1:-1]
        + e_down * w_pad[2:, 1:-1]
        + e_left * w_pad[1:-1, :-2]
        + e_right * w_pad[1:-1, 2:]
    )
    denom = stiffness + e_up + e_down + e_left + e_right
    return numer / denom


def anand(strain, resist, recv):
    total, inelastic = (strain[0], strain[1])
    increment, theta, live = (recv[0], recv[1], recv[2])
    total_new = total + increment
    arrhen = jnp.exp(2.0 - 2.0 / (1.0 + 0.1 * theta * theta))
    hyper = jnp.sinh(shear_mod * (total_new - inelastic) / resist)
    rate = rate_scale * arrhen * hyper * jnp.abs(hyper)
    inelastic_new = inelastic + rate
    target = sat_level * jnp.power(1.0 + jnp.abs(rate) / arrhen, sat_power)
    resist_new = resist + harden * (1.0 - resist / target) * jnp.abs(rate)
    keep = live > 0.5
    strain_out = jnp.stack(
        [jnp.where(keep, total_new, total), jnp.where(keep, inelastic_new, inelastic)]
    )
    return (strain_out, jnp.where(keep, resist_new, resist))


def body(
    temp_start,
    heat_input,
    lateral,
    vertical,
    weighting,
    modulus,
    warp_prev,
    joint_cell,
    joint_owner,
    joint_strain,
    joint_resist,
):
    devices = lax.axis_size(("gx", "gy"))
    temp = temp_start
    for step in range(STEPS):
        ext = with_halo(temp, ((("gx", "gy"), 1),), 1)
        temp = thermal_step(ext, heat_input, lateral, vertical)
    relayed = lax.all_to_all(temp, "gy", split_axis=2, concat_axis=1, tiled=True)
    load = moment_of(relayed, weighting)
    top = relayed[-1]
    e_pad = with_halo(modulus, (("gx", 0), ("gy", 1)), 1)
    warp = warp_prev
    for step in range(SWEEPS):
        w_pad = with_halo(warp, (("gx", 0), ("gy", 1)), 1)
        warp = sweep(w_pad, e_pad, load)
    capacity = joint_resist.shape[1] // devices
    owners = joint_owner[:, 0]
    increment = warp.reshape(-1)[joint_cell] - warp_prev.reshape(-1)[joint_cell]
    theta = top.reshape(-1)[joint_cell]
    values = jnp.stack([increment, theta, jnp.ones_like(theta)])
    onehot = (owners[:, None] == jnp.arange(devices, dtype=jnp.int32)[None, :]).astype(jnp.int32)
    ranks = jnp.sum(jnp.cumsum(onehot, axis=0) * onehot, axis=1) - 1
    slots = owners * capacity + ranks
    outgoing = jnp.zeros((3, devices * capacity), jnp.float32).at[:, slots].set(values)
    incoming = lax.all_to_all(outgoing, ("gx", "gy"), split_axis=1, concat_axis=1, tiled=True)
    strain_next, resist_next = anand(joint_strain, joint_resist, incoming[:, None, :])
    return (warp, strain_next, resist_next)


def solution(mesh):
    return jax.shard_map(
        body,
        mesh=mesh,
        in_specs=(
            P(None, ("gx", "gy"), None),
            P(None, ("gx", "gy"), None),
            P(),
            P(),
            P(),
            P("gx", "gy"),
            P("gx", "gy"),
            P(("gx", "gy")),
            P(("gx", "gy"), None),
            P(None, ("gx", "gy"), None),
            P(("gx", "gy"), None),
        ),
        out_specs=(P("gx", "gy"), P(None, ("gx", "gy"), None), P(("gx", "gy"), None)),
        check_vma=False,
    )
```

profile of v0, /device:TPU:0, one launch (start us, length us, event | category | flops | bytes accessed | tf_op | source)
XLA Modules:
  0.0 217.0 jit_solution(10733385116861195216)
XLA Ops:
  0.6 2.8 %copy.58 = f32[8,32,2048]{2,0,1:T(8,128)S(1)} copy(f32[8,32,2048]{2,1,0:T(8,128)} %param.11) | data formatting | bytes 4194304 | tf_op args[0]
  4.8 5.6 %collective-permute-start.1 = (f32[8,1,2048]{2,0,1:T(8,128)S(1)}, f32[8,1,2048]{2,0,1:T(8,128)S(1)}, u32[]{:S(2)}, u32[]{:S(2)}) collective-permute-start(f32[8,1,2048]{2,0,1:T(8,128)S(1)} %get-tuple-element.11), channel_id=1, source_target_pairs={{0,1},{1,2},{2,3},{3,4},{4,5},{5,6},{6,7},{7,8},{8,9},{9,10},{10,1... | collective-permute-start | bytes 196616 | tf_op jit(solution)/shard_map/ppermute | solution.py:23
  10.8 1.6 collective-permute-done.1
  13.1 2.6 %fusion.13 = f32[8,32,2048]{2,0,1:T(8,128)S(1)} fusion(f32[8,32,2048]{2,0,1:T(8,128)S(1)} %copy.58, f32[8,34,2050]{2,0,1:T(8,128)S(1)} %select_maximum_fusion.2, f32[8,1,2048]{2,0,1:T(8,128)S(1)} %collective-permute-done.1, f32[8,1,2048]{2,0,1:T(8,128)S(1)} %collective-permute-done, f32[7,32,2048]{2,0,1:T(8,128)S(1)} %fusion.8, ...), kind=kLoop, calls=%fused_computation.30 | loop fusion | flops 6291456 | bytes 12451872 | tf_op jit(solution)/shard_map/add | solution.py:35
  17.0 5.0 %collective-permute-start.3 = (f32[8,1,2048]{2,0,1:T(8,128)S(1)}, f32[8,1,2048]{2,0,1:T(8,128)S(1)}, u32[]{:S(2)}, u32[]{:S(2)}) collective-permute-start(f32[8,1,2048]{2,0,1:T(8,128)S(1)} %get-tuple-element.9), channel_id=1, source_target_pairs={{0,1},{1,2},{2,3},{3,4},{4,5},{5,6},{6,7},{7,8},{8,9},{9,10},{10,1... | collective-permute-start | bytes 196616 | tf_op jit(solution)/shard_map/ppermute | solution.py:23
  22.4 1.5 collective-permute-done.3
  24.6 2.6 %fusion.6 = f32[8,32,2048]{2,0,1:T(8,128)S(1)} fusion(f32[8,32,2048]{2,0,1:T(8,128)S(1)} %fusion.13, f32[8,34,2050]{2,0,1:T(8,128)S(1)} %select_maximum_fusion, f32[8,1,2048]{2,0,1:T(8,128)S(1)} %collective-permute-done.3, f32[8,1,2048]{2,0,1:T(8,128)S(1)} %collective-permute-done.2, f32[7,32,2048]{2,0,1:T(8,128)S(1)} %fusion.1, ...), kind=kLoop, calls=%fused_computation.18 | loop fusion | flops 6291456 | bytes 12451872 | tf_op jit(solution)/shard_map/add | solution.py:35
  27.2 4.9 %copy.63 = f32[8,32,2048]{1,0,2:T(8,128)} copy(f32[8,32,2048]{2,0,1:T(8,128)S(1)} %fusion.6) | data formatting | bytes 4194304 | tf_op jit(solution)/shard_map/add | solution.py:35
  32.1 7.1 %reshape.264 = f32[4,1,131072]{2,1,0:T(1,128)} reshape(f32[2048,8,32]{2,1,0:T(8,128)} %bitcast.70) | data formatting | bytes 4194304
  39.2 8.6 %all-to-all-start = ((f32[4,1,131072]{2,1,0:T(1,128)}), f32[4,1,131072]{2,1,0:T(1,128)S(1)}, u32[]{:S(2)}, u32[]{:S(2)}) async-start(f32[4,1,131072]{2,1,0:T(1,128)} %reshape.264), calls=%async_computation | async-start | bytes 4194304 | tf_op jit(solution)/shard_map/all_to_all | solution.py:97
  47.8 4.4 %collective-permute-start.4 = (f32[1,512]{1,0:T(1,128)S(1)}, f32[1,512]{1,0:T(1,128)S(1)}, u32[]{:S(2)}, u32[]{:S(2)}) collective-permute-start(f32[1,512]{1,0:T(1,128)S(1)} %get-tuple-element.26), channel_id=1, source_target_pairs={{0,4},{4,8},{8,12},{12,16},{16,20},{20,24},{24,28},{1,5},{5,9},{9,... | collective-permute-start | bytes 6152 | tf_op jit(solution)/shard_map/ppermute | solution.py:23
  53.6 5.2 %collective-permute-start.5 = (f32[1,512]{1,0:T(1,128)S(1)}, f32[1,512]{1,0:T(1,128)S(1)}, u32[]{:S(2)}, u32[]{:S(2)}) collective-permute-start(f32[1,512]{1,0:T(1,128)S(1)} %get-tuple-element.27), channel_id=1, source_target_pairs={{0,4},{4,8},{8,12},{12,16},{16,20},{20,24},{24,28},{1,5},{5,9},{9,... | collective-permute-start | bytes 6152 | tf_op jit(solution)/shard_map/ppermute | solution.py:23
  60.2 9.1 %reduce-window.6 = s32[32,16,128]{2,1,0:T(8,128)S(1)} reduce-window(s32[32,16,128]{2,1,0:T(8,128)S(1)} %fusion.61, s32[]{:T(128)} %constant.6.clone.1), window={size=1x1x128 pad=0_0x0_0x127_0}, to_apply=%region_0.1 | reduce-window | flops 8323072 | bytes 524292 | tf_op jit(solution)/shard_map/reduce-window
  72.2 4.5 %collective-permute-start.8 = (f32[130,1]{1,0:T(8,128)S(1)}, f32[130,1]{1,0:T(8,128)S(1)}, u32[]{:S(2)}, u32[]{:S(2)}) collective-permute-start(f32[130,1]{1,0:T(8,128)S(1)} %get-tuple-element.18), channel_id=1, source_target_pairs={{0,1},{1,2},{2,3},{4,5},{5,6},{6,7},{8,9},{9,10},{10,11},{12,13},{... | collective-permute-start | bytes 1568 | tf_op jit(solution)/shard_map/ppermute | solution.py:23
  78.7 5.2 %collective-permute-start.9 = (f32[130,1]{1,0:T(8,128)S(1)}, f32[130,1]{1,0:T(8,128)}, u32[]{:S(2)}, u32[]{:S(2)}) collective-permute-start(f32[130,1]{1,0:T(8,128)S(1)} %get-tuple-element.19), channel_id=1, source_target_pairs={{0,1},{1,2},{2,3},{4,5},{5,6},{6,7},{8,9},{9,10},{10,11},{12,13},{... | collective-permute-start | bytes 1568 | tf_op jit(solution)/shard_map/ppermute | solution.py:23
  83.9 12.6 %all-to-all-done = f32[4,1,131072]{2,1,0:T(1,128)S(1)} async-done(((f32[4,1,131072]{2,1,0:T(1,128)}), f32[4,1,131072]{2,1,0:T(1,128)S(1)}, u32[]{:S(2)}, u32[]{:S(2)}) %all-to-all-start) | async-done | bytes 2097184 | tf_op jit(solution)/shard_map/all_to_all | solution.py:97
  98.3 7.7 %reduce.8 = f32[4,131072]{1,0:T(4,128)S(1)} reduce(f32[4,1,131072]{2,1,0:T(1,128)} %copy-done.1, f32[]{:T(128)} %broadcast.270), dimensions={1}, to_apply=%all_to_all.17.reduce_sub_computation | reduce | bytes 4194308 | tf_op jit(solution)/shard_map/all_to_all | solution.py:97
  106.0 6.2 %reshape.265 = f32[2048,8,32]{2,1,0:T(8,128)} reshape(f32[4,131072]{1,0:T(4,128)S(1)} %reduce.8) | data formatting | bytes 4194304
  112.2 5.1 %copy.64 = f32[8,32,4,512]{3,1,2,0:T(8,128)S(1)} copy(f32[8,32,4,512]{1,0,3,2:T(8,128)} %bitcast.71) | data formatting | bytes 4194304 | tf_op jit(solution)/shard_map/all_to_all | solution.py:97
  117.3 5.2 %fusion.72 = (f32[1,4,32,512]{3,2,1,0:T(8,128)S(1)}, f32[1,4,32,512]{3,2,1,0:T(8,128)S(1)}) fusion(f32[8,4,32,512]{3,2,1,0:T(8,128)S(1)} %bitcast.73, f32[]{:T(128)} %bitcast.9, f32[]{:T(128)} %bitcast.8, f32[]{:T(128)} %bitcast.7, f32[]{:T(128)} %bitcast.6, f32[]{:T(128)} %bitcast.5, f32[]{:T(128)} %bitcast.4, f32[]{:T(128)} %bitcast.3, f32[]{:T(128)} %bitcast), kind=kLoop, calls=%fused_computation.165 | loop fusion | flops 983040 | bytes 2621472 | tf_op jit(solution)/shard_map/slice | solution.py:41
  123.9 3.7 %collective-permute-start.12 = (f32[1,512]{1,0:T(1,128)S(1)}, f32[1,512]{1,0:T(1,128)S(1)}, u32[]{:S(2)}, u32[]{:S(2)}) collective-permute-start(f32[1,512]{1,0:T(1,128)S(1)} %get-tuple-element.23), channel_id=1, source_target_pairs={{0,4},{4,8},{8,12},{12,16},{16,20},{20,24},{24,28},{1,5},{5,9},{9,... | collective-permute-start | bytes 6152 | tf_op jit(solution)/shard_map/ppermute | solution.py:23
  128.9 4.2 %collective-permute-done.13 = f32[1,512]{1,0:T(1,128)S(1)} collective-permute-done((f32[1,512]{1,0:T(1,128)S(1)}, f32[1,512]{1,0:T(1,128)S(1)}, u32[]{:S(2)}, u32[]{:S(2)}) %collective-permute-start.13) | collective-permute-done | bytes 2080 | tf_op jit(solution)/shard_map/ppermute | solution.py:24
  136.4 4.3 %collective-permute-done.15 = f32[130,1]{1,0:T(8,128)S(1)} collective-permute-done((f32[130,1]{1,0:T(8,128)S(1)}, f32[130,1]{1,0:T(8,128)S(1)}, u32[]{:S(2)}, u32[]{:S(2)}) %collective-permute-start.15) | collective-permute-done | bytes 552 | tf_op jit(solution)/shard_map/ppermute | solution.py:24
  141.1 3.1 %collective-permute-start.16 = (f32[1,512]{1,0:T(1,128)S(1)}, f32[1,512]{1,0:T(1,128)S(1)}, u32[]{:S(2)}, u32[]{:S(2)}) collective-permute-start(f32[1,512]{1,0:T(1,128)S(1)} %get-tuple-element.21), channel_id=1, source_target_pairs={{0,4},{4,8},{8,12},{12,16},{16,20},{20,24},{24,28},{1,5},{5,9},{9,... | collective-permute-start | bytes 6152 | tf_op jit(solution)/shard_map/ppermute | solution.py:23
  145.6 11.8 %gather_fusion.1 = f32[2048]{0:T(1024)S(1)} fusion(f32[65536]{0:T(1024)S(1)} %bitcast.69, s32[2048]{0:T(1024)S(1)} %fusion.71), kind=kCustom, calls=%fused_computation.1 | custom fusion | bytes 24576 | tf_op jit(solution)/shard_map/gather | solution.py:107
  157.5 3.6 %collective-permute-start.18 = (f32[130,1]{1,0:T(8,128)S(1)}, f32[130,1]{1,0:T(8,128)S(1)}, u32[]{:S(2)}, u32[]{:S(2)}) collective-permute-start(f32[130,1]{1,0:T(8,128)S(1)} %get-tuple-element.13), channel_id=1, source_target_pairs={{0,1},{1,2},{2,3},{4,5},{5,6},{6,7},{8,9},{9,10},{10,11},{12,13},{... | collective-permute-start | bytes 1568 | tf_op jit(solution)/shard_map/ppermute | solution.py:23
  161.2 1.5 collective-permute-start.19
  162.8 11.8 %gather_fusion.2 = f32[2048]{0:T(1024)S(1)} fusion(f32[65536]{0:T(1024)S(1)} %bitcast.67, s32[2048]{0:T(1024)S(1)} %fusion.71), kind=kCustom, calls=%fused_computation.2 | custom fusion | bytes 24576 | tf_op jit(solution)/shard_map/gather | solution.py:108
  175.2 11.8 %gather_fusion = f32[2048]{0:T(1024)S(1)} fusion(f32[65536]{0:T(1024)S(1)} %bitcast.68, s32[2048]{0:T(1024)S(1)} %fusion.71), kind=kCustom, calls=%fused_computation | custom fusion | bytes 24576 | tf_op jit(solution)/shard_map/gather | solution.py:107
  188.4 6.7 %scatter_custom_fusion = f32[3,6144]{0,1:T(8,128)S(1)} fusion(s32[2048]{0:T(1024)} %bitcast.85, f32[2048,3]{1,0:T(8,128)} %copy.67, f32[]{:T(128)} %constant.16.clone.1), kind=kCustom, calls=%fused_computation.35 | custom fusion | bytes 74240 | tf_op jit(solution)/shard_map/scatter | solution.py:113
  195.2 1.5 copy.68
  196.6 17.7 %all_to_all.24 = f32[3,32,192]{2,0,1:T(4,128)S(1)} all-to-all(f32[3,32,192]{2,0,1:T(4,128)S(1)} %copy.68), channel_id=1, replica_groups=mesh['gx'=8,'gy'=4] {'gx','gy'}, dimensions={1} | all-to-all | bytes 147456 | tf_op jit(solution)/shard_map/all_to_all | solution.py:114
  (96 shorter events, 26.6 us)
Async XLA Ops:
  0.6 9.7 %copy-start.10 = (f32[7]{0:T(128)S(1)}, f32[7]{0:T(128)}, u32[]{:S(2)}) copy-start(f32[7]{0:T(128)} %param.14) | copy-start | bytes 88
  3.5 7.3 %collective-permute-start = (f32[8,1,2048]{2,0,1:T(8,128)S(1)}, f32[8,1,2048]{2,0,1:T(8,128)S(1)}, u32[]{:S(2)}, u32[]{:S(2)}) collective-permute-start(f32[8,1,2048]{2,0,1:T(8,128)S(1)} %get-tuple-element.12), channel_id=1, source_target_pairs={{1,0},{2,1},{3,2},{4,3},{5,4},{6,5},{7,6},{8,7},{9,8},{10,9},{11,1... | collective-permute-start | bytes 196616 | tf_op jit(solution)/shard_map/ppermute | solution.py:24
  4.8 7.6 %collective-permute-start.1 = (f32[8,1,2048]{2,0,1:T(8,128)S(1)}, f32[8,1,2048]{2,0,1:T(8,128)S(1)}, u32[]{:S(2)}, u32[]{:S(2)}) collective-permute-start(f32[8,1,2048]{2,0,1:T(8,128)S(1)} %get-tuple-element.11), channel_id=1, source_target_pairs={{0,1},{1,2},{2,3},{3,4},{4,5},{5,6},{6,7},{7,8},{8,9},{9,10},{10,1... | collective-permute-start | bytes 196616 | tf_op jit(solution)/shard_map/ppermute | solution.py:23
  10.8 2.3 %copy-start = (f32[8,32,2048]{2,1,0:T(8,128)S(1)}, f32[8,32,2048]{2,1,0:T(8,128)}, u32[]{:S(2)}) copy-start(f32[8,32,2048]{2,1,0:T(8,128)} %param.12) | copy-start | bytes 6291460
  10.8 2.3 %copy-start.11 = (f32[8]{0:T(128)S(1)}, f32[8]{0:T(128)}, u32[]{:S(2)}) copy-start(f32[8]{0:T(128)} %param.13) | copy-start | bytes 100
  15.7 6.7 %collective-permute-start.2 = (f32[8,1,2048]{2,0,1:T(8,128)S(1)}, f32[8,1,2048]{2,0,1:T(8,128)S(1)}, u32[]{:S(2)}, u32[]{:S(2)}) collective-permute-start(f32[8,1,2048]{2,0,1:T(8,128)S(1)} %get-tuple-element.10), channel_id=1, source_target_pairs={{1,0},{2,1},{3,2},{4,3},{5,4},{6,5},{7,6},{8,7},{9,8},{10,9},{11,1... | collective-permute-start | bytes 196616 | tf_op jit(solution)/shard_map/ppermute | solution.py:24
  17.0 6.9 %collective-permute-start.3 = (f32[8,1,2048]{2,0,1:T(8,128)S(1)}, f32[8,1,2048]{2,0,1:T(8,128)S(1)}, u32[]{:S(2)}, u32[]{:S(2)}) collective-permute-start(f32[8,1,2048]{2,0,1:T(8,128)S(1)} %get-tuple-element.9), channel_id=1, source_target_pairs={{0,1},{1,2},{2,3},{3,4},{4,5},{5,6},{6,7},{7,8},{8,9},{9,10},{10,1... | collective-permute-start | bytes 196616 | tf_op jit(solution)/shard_map/ppermute | solution.py:23
  39.2 8.6 %copy-start.2 = (f32[128,512]{1,0:T(8,128)S(1)}, f32[128,512]{1,0:T(8,128)}, u32[]{:S(2)}) copy-start(f32[128,512]{1,0:T(8,128)} %param.16) | copy-start | bytes 786436
  39.2 14.4 %copy-start.3 = (f32[128,512]{1,0:T(8,128)S(1)}, f32[128,512]{1,0:T(8,128)}, u32[]{:S(2)}) copy-start(f32[128,512]{1,0:T(8,128)} %param.17) | copy-start | bytes 786436
  39.2 20.9 %copy-start.6 = (s32[2048,1]{0,1:T(1,128)S(1)}, s32[2048,1]{0,1:T(1,128)}, u32[]{:S(2)}) copy-start(s32[2048,1]{0,1:T(1,128)} %param.19) | copy-start | bytes 24580
  39.2 57.2 %all-to-all-start = ((f32[4,1,131072]{2,1,0:T(1,128)}), f32[4,1,131072]{2,1,0:T(1,128)S(1)}, u32[]{:S(2)}, u32[]{:S(2)}) async-start(f32[4,1,131072]{2,1,0:T(1,128)} %reshape.264), calls=%async_computation | async-start | bytes 4194304 | tf_op jit(solution)/shard_map/all_to_all | solution.py:97
  47.8 22.3 %copy-start.7 = (f32[8]{0:T(128)S(1)}, f32[8]{0:T(128)}, u32[]{:S(2)}) copy-start(f32[8]{0:T(128)} %param.15) | copy-start | bytes 100
  47.8 22.9 %collective-permute-start.4 = (f32[1,512]{1,0:T(1,128)S(1)}, f32[1,512]{1,0:T(1,128)S(1)}, u32[]{:S(2)}, u32[]{:S(2)}) collective-permute-start(f32[1,512]{1,0:T(1,128)S(1)} %get-tuple-element.26), channel_id=1, source_target_pairs={{0,4},{4,8},{8,12},{12,16},{16,20},{20,24},{24,28},{1,5},{5,9},{9,... | collective-permute-start | bytes 6152 | tf_op jit(solution)/shard_map/ppermute | solution.py:23
  52.3 18.5 %collective-permute-start.6 = (f32[1,512]{1,0:T(1,128)S(1)}, f32[1,512]{1,0:T(1,128)S(1)}, u32[]{:S(2)}, u32[]{:S(2)}) collective-permute-start(f32[1,512]{1,0:T(1,128)S(1)} %get-tuple-element.25), channel_id=1, source_target_pairs={{4,0},{8,4},{12,8},{16,12},{20,16},{24,20},{28,24},{5,1},{9,5},{13... | collective-permute-start | bytes 6152 | tf_op jit(solution)/shard_map/ppermute | solution.py:24
  53.6 23.1 %collective-permute-start.5 = (f32[1,512]{1,0:T(1,128)S(1)}, f32[1,512]{1,0:T(1,128)S(1)}, u32[]{:S(2)}, u32[]{:S(2)}) collective-permute-start(f32[1,512]{1,0:T(1,128)S(1)} %get-tuple-element.27), channel_id=1, source_target_pairs={{0,4},{4,8},{8,12},{12,16},{16,20},{20,24},{24,28},{1,5},{5,9},{9,... | collective-permute-start | bytes 6152 | tf_op jit(solution)/shard_map/ppermute | solution.py:23
  58.8 17.9 %collective-permute-start.7 = (f32[1,512]{1,0:T(1,128)S(1)}, f32[1,512]{1,0:T(1,128)S(1)}, u32[]{:S(2)}, u32[]{:S(2)}) collective-permute-start(f32[1,512]{1,0:T(1,128)S(1)} %get-tuple-element.28), channel_id=1, source_target_pairs={{4,0},{8,4},{12,8},{16,12},{20,16},{24,20},{28,24},{5,1},{9,5},{13... | collective-permute-start | bytes 6152 | tf_op jit(solution)/shard_map/ppermute | solution.py:24
  70.9 51.6 %collective-permute-start.10 = (f32[130,1]{1,0:T(8,128)S(1)}, f32[130,1]{1,0:T(8,128)S(1)}, u32[]{:S(2)}, u32[]{:S(2)}) collective-permute-start(f32[130,1]{1,0:T(8,128)S(1)} %get-tuple-element.17), channel_id=1, source_target_pairs={{1,0},{2,1},{3,2},{5,4},{6,5},{7,6},{9,8},{10,9},{11,10},{13,12},{... | collective-permute-start | bytes 1568 | tf_op jit(solution)/shard_map/ppermute | solution.py:24
  72.2 50.3 %collective-permute-start.8 = (f32[130,1]{1,0:T(8,128)S(1)}, f32[130,1]{1,0:T(8,128)S(1)}, u32[]{:S(2)}, u32[]{:S(2)}) collective-permute-start(f32[130,1]{1,0:T(8,128)S(1)} %get-tuple-element.18), channel_id=1, source_target_pairs={{0,1},{1,2},{2,3},{4,5},{5,6},{6,7},{8,9},{9,10},{10,11},{12,13},{... | collective-permute-start | bytes 1568 | tf_op jit(solution)/shard_map/ppermute | solution.py:23
  77.4 45.1 %collective-permute-start.11 = (f32[130,1]{1,0:T(8,128)}, f32[130,1]{1,0:T(8,128)}, u32[]{:S(2)}, u32[]{:S(2)}) collective-permute-start(f32[130,1]{1,0:T(8,128)} %get-tuple-element.20), channel_id=1, source_target_pairs={{1,0},{2,1},{3,2},{5,4},{6,5},{7,6},{9,8},{10,9},{11,10},{13,12},{... | collective-permute-start | bytes 1568 | tf_op jit(solution)/shard_map/ppermute | solution.py:24
  78.7 43.8 %collective-permute-start.9 = (f32[130,1]{1,0:T(8,128)S(1)}, f32[130,1]{1,0:T(8,128)}, u32[]{:S(2)}, u32[]{:S(2)}) collective-permute-start(f32[130,1]{1,0:T(8,128)S(1)} %get-tuple-element.19), channel_id=1, source_target_pairs={{0,1},{1,2},{2,3},{4,5},{5,6},{6,7},{8,9},{9,10},{10,11},{12,13},{... | collective-permute-start | bytes 1568 | tf_op jit(solution)/shard_map/ppermute | solution.py:23
  122.5 23.0 %copy-start.9 = (s32[2048]{0:T(1024)S(1)}, s32[2048]{0:T(1024)}, u32[]{:S(2)}) copy-start(s32[2048]{0:T(1024)} %param.18) | copy-start | bytes 24580
  123.9 5.0 %collective-permute-start.12 = (f32[1,512]{1,0:T(1,128)S(1)}, f32[1,512]{1,0:T(1,128)S(1)}, u32[]{:S(2)}, u32[]{:S(2)}) collective-permute-start(f32[1,512]{1,0:T(1,128)S(1)} %get-tuple-element.23), channel_id=1, source_target_pairs={{0,4},{4,8},{8,12},{12,16},{16,20},{20,24},{24,28},{1,5},{5,9},{9,... | collective-permute-start | bytes 6152 | tf_op jit(solution)/shard_map/ppermute | solution.py:23
  127.6 5.5 %collective-permute-start.13 = (f32[1,512]{1,0:T(1,128)S(1)}, f32[1,512]{1,0:T(1,128)S(1)}, u32[]{:S(2)}, u32[]{:S(2)}) collective-permute-start(f32[1,512]{1,0:T(1,128)S(1)} %get-tuple-element.24), channel_id=1, source_target_pairs={{4,0},{8,4},{12,8},{16,12},{20,16},{24,20},{28,24},{5,1},{9,5},{13... | collective-permute-start | bytes 6152 | tf_op jit(solution)/shard_map/ppermute | solution.py:24
  133.2 3.2 %collective-permute-start.14 = (f32[130,1]{1,0:T(8,128)S(1)}, f32[130,1]{1,0:T(8,128)S(1)}, u32[]{:S(2)}, u32[]{:S(2)}) collective-permute-start(f32[130,1]{1,0:T(8,128)S(1)} %get-tuple-element.15), channel_id=1, source_target_pairs={{0,1},{1,2},{2,3},{4,5},{5,6},{6,7},{8,9},{9,10},{10,11},{12,13},{... | collective-permute-start | bytes 1568 | tf_op jit(solution)/shard_map/ppermute | solution.py:23
  134.5 6.2 %collective-permute-start.15 = (f32[130,1]{1,0:T(8,128)S(1)}, f32[130,1]{1,0:T(8,128)S(1)}, u32[]{:S(2)}, u32[]{:S(2)}) collective-permute-start(f32[130,1]{1,0:T(8,128)S(1)} %get-tuple-element.16), channel_id=1, source_target_pairs={{1,0},{2,1},{3,2},{5,4},{6,5},{7,6},{9,8},{10,9},{11,10},{13,12},{... | collective-permute-start | bytes 1568 | tf_op jit(solution)/shard_map/ppermute | solution.py:24
  141.1 16.3 %collective-permute-start.16 = (f32[1,512]{1,0:T(1,128)S(1)}, f32[1,512]{1,0:T(1,128)S(1)}, u32[]{:S(2)}, u32[]{:S(2)}) collective-permute-start(f32[1,512]{1,0:T(1,128)S(1)} %get-tuple-element.21), channel_id=1, source_target_pairs={{0,4},{4,8},{8,12},{12,16},{16,20},{20,24},{24,28},{1,5},{5,9},{9,... | collective-permute-start | bytes 6152 | tf_op jit(solution)/shard_map/ppermute | solution.py:23
  144.2 13.2 %collective-permute-start.17 = (f32[1,512]{1,0:T(1,128)S(1)}, f32[1,512]{1,0:T(1,128)S(1)}, u32[]{:S(2)}, u32[]{:S(2)}) collective-permute-start(f32[1,512]{1,0:T(1,128)S(1)} %get-tuple-element.22), channel_id=1, source_target_pairs={{4,0},{8,4},{12,8},{16,12},{20,16},{24,20},{28,24},{5,1},{9,5},{13... | collective-permute-start | bytes 6152 | tf_op jit(solution)/shard_map/ppermute | solution.py:24
  157.5 17.1 %collective-permute-start.18 = (f32[130,1]{1,0:T(8,128)S(1)}, f32[130,1]{1,0:T(8,128)S(1)}, u32[]{:S(2)}, u32[]{:S(2)}) collective-permute-start(f32[130,1]{1,0:T(8,128)S(1)} %get-tuple-element.13), channel_id=1, source_target_pairs={{0,1},{1,2},{2,3},{4,5},{5,6},{6,7},{8,9},{9,10},{10,11},{12,13},{... | collective-permute-start | bytes 1568 | tf_op jit(solution)/shard_map/ppermute | solution.py:23
  161.2 13.5 %collective-permute-start.19 = (f32[130,1]{1,0:T(8,128)S(1)}, f32[130,1]{1,0:T(8,128)S(1)}, u32[]{:S(2)}, u32[]{:S(2)}) collective-permute-start(f32[130,1]{1,0:T(8,128)S(1)} %get-tuple-element.14), channel_id=1, source_target_pairs={{1,0},{2,1},{3,2},{5,4},{6,5},{7,6},{9,8},{10,9},{11,10},{13,12},{... | collective-permute-start | bytes 1568 | tf_op jit(solution)/shard_map/ppermute | solution.py:24
  175.1 11.9 %copy-start.4 = (f32[128,512]{1,0:T(8,128)}, f32[128,512]{1,0:T(8,128)S(1)}, u32[]{:S(2)}) copy-start(f32[128,512]{1,0:T(8,128)S(1)} %fusion.21) | copy-start | bytes 786436
  195.2 20.0 %copy-start.5 = (f32[2,1,6144]{2,1,0:T(1,128)S(1)}, f32[2,1,6144]{2,1,0:T(1,128)}, u32[]{:S(2)}) copy-start(f32[2,1,6144]{2,1,0:T(1,128)} %param.20) | copy-start | bytes 147460
  195.2 20.0 %copy-start.8 = (f32[1,6144]{1,0:T(1,128)S(1)}, f32[1,6144]{1,0:T(1,128)}, u32[]{:S(2)}) copy-start(f32[1,6144]{1,0:T(1,128)} %param.21) | copy-start | bytes 73732
  (1 other events, 1.3 us)
where the time goes:
time: 218 us; the launch traced here: 217 us
  local copies, waits for them, and re-layouts  75 us (34%)
  starting transfers between devices  63.5 us (29%)
  other arithmetic  35.5 us (16%)
  waiting for transfers between devices  24.1 us (11%)
  blocking collectives  17.7 us (8%)
    ppermute x10, starting transfers between devices, with_halo(): before = lax.ppermute(last, axis, up)  41.7 us
    gather x2, local copies, waits for them, and re-layouts, body(): increment = warp.reshape(-1)[joint_cell] - warp_prev.reshape(-1)[joint_cell]  23.6 us
    all_to_all x1, blocking collectives, body(): lax.all_to_all(outgoing, ('gx', 'gy'), split_axis=1, concat_axis=1, tiled...  17.7 us
    unnamed x30, local copies, waits for them, and re-layouts  17.7 us
    ppermute x10, starting transfers between devices, with_halo(): after = lax.ppermute(leading, axis, down)  13.1 us
    all_to_all x1, waiting for transfers between devices, body(): lax.all_to_all(temp, 'gy', split_axis=2, concat_axis=1, tiled=True)  12.6 us
    gather x1, local copies, waits for them, and re-layouts, body(): theta = top.reshape(-1)[joint_cell]  11.8 us
    another operation x3, other arithmetic  9.41 us
  transfers between devices with their start and end apart: 21, of which 5 were waited for; matrix products, arithmetic and copies ran while one was open for 28% of the time, Pallas kernels for 0%

commit v1 on v0

--- a/solution.py
+++ b/solution.py
@@ -11,6 +11,22 @@
 sat_level = 2.5
 sat_power = 0.3
 harden = 2.0
+
+
+def swapped_with_each(x, axis, split, join):
+    ways, here = (lax.axis_size(axis), lax.axis_index(axis))
+    width = x.shape[split] // ways
+    lengths = list(x.shape)
+    lengths[split] = width
+    height = lengths[join]
+    lengths[join] = height * ways
+    full = jnp.zeros(lengths, x.dtype)
+    for mask in range(ways):
+        part = lax.dynamic_slice_in_dim(x, (here ^ mask) * width, width, axis=split)
+        if mask:
+            part = lax.ppermute(part, axis, [(d, d ^ mask) for d in range(ways)])
+        full = lax.dynamic_update_slice_in_dim(full, part, (here ^ mask) * height, axis=join)
+    return full
 
 
 def with_halo(array, sides, width):
@@ -94,7 +110,7 @@
     for step in range(STEPS):
         ext = with_halo(temp, ((("gx", "gy"), 1),), 1)
         temp = thermal_step(ext, heat_input, lateral, vertical)
-    relayed = lax.all_to_all(temp, "gy", split_axis=2, concat_axis=1, tiled=True)
+    relayed = swapped_with_each(temp, "gy", 2, 1)
     load = moment_of(relayed, weighting)
     top = relayed[-1]
     e_pad = with_halo(modulus, (("gx", 0), ("gy", 1)), 1)

time: 218 us -> 211 us (0.968)
  local copies, waits for them, and re-layouts: 75 us -> 63.8 us
  waiting for transfers between devices: 24.1 us -> 34.8 us
  other arithmetic: 35.5 us -> 30.5 us
    ppermute x0 -> x3, waiting for transfers between devices: none -> 18.2 us  [swapped_with_each(): part = lax.ppermute(part, axis, [(d, d ^ mask) for d in range(ways)])]
    unnamed x30 -> x40, local copies, waits for them, and re-layouts: 17.7 us -> 2 us
    all_to_all x1 -> x0, waiting for transfers between devices: 12.6 us -> none  [body(): lax.all_to_all(temp, 'gy', split_axis=2, concat_axis=1, tiled=True)]
    gather x2, local copies, waits for them, and re-layouts: 23.6 us -> 32.3 us  [body(): increment = warp.reshape(-1)[joint_cell] - warp_prev.reshape(-1)[joint_cell]]
    all_to_all x1 -> x0, starting transfers between devices: 8.62 us -> none  [body(): lax.all_to_all(temp, 'gy', split_axis=2, concat_axis=1, tiled=True)]
    all_to_all x1 -> x0, other arithmetic: 7.72 us -> none  [body(): lax.all_to_all(temp, 'gy', split_axis=2, concat_axis=1, tiled=True)]
    ppermute x10, waiting for transfers between devices: 8.46 us -> 14.9 us  [with_halo(): after = lax.ppermute(leading, axis, down)]
    ppermute x0 -> x3, starting transfers between devices: none -> 6.14 us  [swapped_with_each(): part = lax.ppermute(part, axis, [(d, d ^ mask) for d in range(ways)])]
  transfers between devices with their start and end apart: 21 -> 23, of which waited for: 5 -> 7; matrix products, arithmetic and copies ran while one was open for 28% -> 28% of each run, Pallas kernels for 0% -> 0%
where the time goes in v1:
time: 211 us; the launch traced here: 210 us
  local copies, waits for them, and re-layouts  63.8 us (30%)
  starting transfers between devices  63.7 us (30%)
  waiting for transfers between devices  34.8 us (16%)
  other arithmetic  30.5 us (14%)
  blocking collectives  16.3 us (8%)
    ppermute x10, starting transfers between devices, with_halo(): before = lax.ppermute(last, axis, up)  44.5 us
    gather x2, local copies, waits for them, and re-layouts, body(): increment = warp.reshape(-1)[joint_cell] - warp_prev.reshape(-1)[joint_cell]  32.3 us
    ppermute x3, waiting for transfers between devices, swapped_with_each(): part = lax.ppermute(part, axis, [(d, d ^ mask) for d in range(ways)])  18.2 us
    all_to_all x1, blocking collectives, body(): lax.all_to_all(outgoing, ('gx', 'gy'), split_axis=1, concat_axis=1, tiled...  16.3 us
    ppermute x10, waiting for transfers between devices, with_halo(): after = lax.ppermute(leading, axis, down)  14.9 us
    ppermute x10, starting transfers between devices, with_halo(): after = lax.ppermute(leading, axis, down)  13.1 us
    gather x1, local copies, waits for them, and re-layouts, body(): theta = top.reshape(-1)[joint_cell]  11.8 us
    another operation x3, other arithmetic  9.41 us
  transfers between devices with their start and end apart: 23, of which 7 were waited for; matrix products, arithmetic and copies ran while one was open for 28% of the time, Pallas kernels for 0%

profile of v1, /device:TPU:0, one launch (start us, length us, event | category | flops | bytes accessed | tf_op | source)
XLA Modules:
  0.0 210.5 jit_solution(10876824078558867096)
XLA Ops:
  3.2 5.6 %collective-permute-start.1 = (f32[8,1,2048]{2,1,0:T(1,128)S(1)}, f32[8,1,2048]{2,1,0:T(1,128)S(1)}, u32[]{:S(2)}, u32[]{:S(2)}) collective-permute-start(f32[8,1,2048]{2,1,0:T(1,128)S(1)} %get-tuple-element.15), channel_id=1, source_target_pairs={{0,1},{1,2},{2,3},{3,4},{4,5},{5,6},{6,7},{7,8},{8,9},{9,10},{10,1... | collective-permute-start | bytes 196616 | tf_op jit(solution)/shard_map/ppermute | solution.py:39
  9.6 4.0 %collective-permute-start.7 = (f32[1,512]{1,0:T(1,128)S(1)}, f32[1,512]{1,0:T(1,128)S(1)}, u32[]{:S(2)}, u32[]{:S(2)}) collective-permute-start(f32[1,512]{1,0:T(1,128)S(1)} %get-tuple-element.30), channel_id=1, source_target_pairs={{0,4},{4,8},{8,12},{12,16},{16,20},{20,24},{24,28},{1,5},{5,9},{9,... | collective-permute-start | bytes 6152 | tf_op jit(solution)/shard_map/ppermute | solution.py:39
  14.9 3.9 %subtract_multiply_fusion = f32[7,32,2048]{2,1,0:T(8,128)} fusion(f32[8,32,2048]{2,1,0:T(8,128)} %param.11, f32[7]{0:T(128)} %param.14), kind=kLoop, calls=%fused_computation.33 | loop fusion | flops 917504 | bytes 5505052 | tf_op jit(solution)/shard_map/mul | solution.py:49
  18.8 9.1 %reduce-window.6 = s32[32,16,128]{2,1,0:T(8,128)S(1)} reduce-window(s32[32,16,128]{2,1,0:T(8,128)S(1)} %fusion.61, s32[]{:T(128)} %constant.26.clone.1), window={size=1x1x128 pad=0_0x0_0x127_0}, to_apply=%region_0.1 | reduce-window | flops 8323072 | bytes 524292 | tf_op jit(solution)/shard_map/reduce-window
  30.8 1.9 fusion.11
  34.1 4.5 %collective-permute-start.3 = (f32[8,1,2048]{2,1,0:T(1,128)S(1)}, f32[8,1,2048]{2,1,0:T(1,128)S(1)}, u32[]{:S(2)}, u32[]{:S(2)}) collective-permute-start(f32[8,1,2048]{2,1,0:T(1,128)S(1)} %get-tuple-element.13), channel_id=1, source_target_pairs={{0,1},{1,2},{2,3},{3,4},{4,5},{5,6},{6,7},{7,8},{8,9},{9,10},{10,1... | collective-permute-start | bytes 196616 | tf_op jit(solution)/shard_map/ppermute | solution.py:39
  39.1 1.7 collective-permute-done.3
  41.8 1.9 fusion.5
  45.2 2.5 %collective-permute-start.4 = (f32[8,32,512]{2,1,0:T(8,128)}, f32[8,32,512]{2,1,0:T(8,128)}, u32[]{:S(2)}, u32[]{:S(2)}) collective-permute-start(f32[8,32,512]{2,1,0:T(8,128)} %get-tuple-element.11), channel_id=1, source_target_pairs={{0,1},{1,0},{2,3},{3,2},{4,5},{5,4},{6,7},{7,6},{8,9},{9,8},{10,11... | collective-permute-start | bytes 1572872 | tf_op jit(solution)/shard_map/ppermute | solution.py:27
  47.7 3.6 %collective-permute-start.5 = (f32[8,32,512]{2,1,0:T(8,128)}, f32[8,32,512]{2,1,0:T(8,128)}, u32[]{:S(2)}, u32[]{:S(2)}) collective-permute-start(f32[8,32,512]{2,1,0:T(8,128)} %get-tuple-element.10), channel_id=1, source_target_pairs={{0,2},{1,3},{2,0},{3,1},{4,6},{5,7},{6,4},{7,5},{8,10},{9,11},{10,... | collective-permute-start | bytes 1572872 | tf_op jit(solution)/shard_map/ppermute | solution.py:27
  53.5 5.7 %collective-permute-start.8 = (f32[1,512]{1,0:T(1,128)S(1)}, f32[1,512]{1,0:T(1,128)S(1)}, u32[]{:S(2)}, u32[]{:S(2)}) collective-permute-start(f32[1,512]{1,0:T(1,128)S(1)} %get-tuple-element.31), channel_id=1, source_target_pairs={{0,4},{4,8},{8,12},{12,16},{16,20},{20,24},{24,28},{1,5},{5,9},{9,... | collective-permute-start | bytes 6152 | tf_op jit(solution)/shard_map/ppermute | solution.py:39
  59.2 1.3 collective-permute-start.11
  61.9 5.3 %collective-permute-done.4 = f32[8,32,512]{2,1,0:T(8,128)} collective-permute-done((f32[8,32,512]{2,1,0:T(8,128)}, f32[8,32,512]{2,1,0:T(8,128)}, u32[]{:S(2)}, u32[]{:S(2)}) %collective-permute-start.4) | collective-permute-done | bytes 524320 | tf_op jit(solution)/shard_map/ppermute | solution.py:27
  67.2 1.4 collective-permute-start.12
  72.2 12.9 %collective-permute-done.6 = f32[8,32,512]{2,1,0:T(8,128)S(1)} collective-permute-done((f32[8,32,512]{2,1,0:T(8,128)}, f32[8,32,512]{2,1,0:T(8,128)S(1)}, u32[]{:S(2)}, u32[]{:S(2)}) %collective-permute-start.6) | collective-permute-done | bytes 524320 | tf_op jit(solution)/shard_map/ppermute | solution.py:27
  85.1 3.4 %collective-permute-done.14 = f32[130,1]{1,0:T(8,128)S(1)} collective-permute-done((f32[130,1]{1,0:T(8,128)S(1)}, f32[130,1]{1,0:T(8,128)S(1)}, u32[]{:S(2)}, u32[]{:S(2)}) %collective-permute-start.14) | collective-permute-done | bytes 552 | tf_op jit(solution)/shard_map/ppermute | solution.py:40
  88.6 5.4 %fusion.38 = (f32[128,512]{1,0:T(8,128)S(1)}, f32[128,512]{1,0:T(8,128)S(1)}) fusion(f32[130,1]{1,0:T(8,128)S(1)} %collective-permute-done.14, f32[1,512]{1,0:T(1,128)S(1)} %collective-permute-done.10, f32[128,512]{1,0:T(8,128)S(1)} %copy-done.4, f32[1,512]{1,0:T(1,128)S(1)} %collective-permute-done.8, f32[130,1]{1,0:T(8,128)S(1)} %collective-permute-done.12, ...), kind=kLoop, calls=%fused_computation.77 | loop fusion | flops 3407872 | bytes 3156032 | tf_op jit(solution)/shard_map/div | solution.py:75
  94.0 6.6 %collective-permute-start.15 = (f32[1,512]{1,0:T(1,128)S(1)}, f32[1,512]{1,0:T(1,128)S(1)}, u32[]{:S(2)}, u32[]{:S(2)}) collective-permute-start(f32[1,512]{1,0:T(1,128)S(1)} %get-tuple-element.27), channel_id=1, source_target_pairs={{0,4},{4,8},{8,12},{12,16},{16,20},{20,24},{24,28},{1,5},{5,9},{9,... | collective-permute-start | bytes 6152 | tf_op jit(solution)/shard_map/ppermute | solution.py:39
  101.9 7.1 %collective-permute-done.16 = f32[1,512]{1,0:T(1,128)S(1)} collective-permute-done((f32[1,512]{1,0:T(1,128)S(1)}, f32[1,512]{1,0:T(1,128)S(1)}, u32[]{:S(2)}, u32[]{:S(2)}) %collective-permute-start.16) | collective-permute-done | bytes 2080 | tf_op jit(solution)/shard_map/ppermute | solution.py:40
  109.1 9.5 %collective-permute-start.17 = (f32[130,1]{1,0:T(8,128)S(1)}, f32[130,1]{1,0:T(8,128)S(1)}, u32[]{:S(2)}, u32[]{:S(2)}) collective-permute-start(f32[130,1]{1,0:T(8,128)S(1)} %get-tuple-element.19), channel_id=1, source_target_pairs={{0,1},{1,2},{2,3},{4,5},{5,6},{6,7},{8,9},{9,10},{10,11},{12,13},{... | collective-permute-start | bytes 1568 | tf_op jit(solution)/shard_map/ppermute | solution.py:39
  120.5 4.3 %collective-permute-done.18 = f32[130,1]{1,0:T(8,128)S(1)} collective-permute-done((f32[130,1]{1,0:T(8,128)S(1)}, f32[130,1]{1,0:T(8,128)S(1)}, u32[]{:S(2)}, u32[]{:S(2)}) %collective-permute-start.18) | collective-permute-done | bytes 552 | tf_op jit(solution)/shard_map/ppermute | solution.py:40
  125.9 3.4 %collective-permute-start.19 = (f32[1,512]{1,0:T(1,128)}, f32[1,512]{1,0:T(1,128)}, u32[]{:S(2)}, u32[]{:S(2)}) collective-permute-start(f32[1,512]{1,0:T(1,128)} %get-tuple-element.25), channel_id=1, source_target_pairs={{0,4},{4,8},{8,12},{12,16},{16,20},{20,24},{24,28},{1,5},{5,9},{9,... | collective-permute-start | bytes 6152 | tf_op jit(solution)/shard_map/ppermute | solution.py:39
  130.7 20.6 %gather_fusion.1 = f32[2048]{0:T(1024)} fusion(f32[65536]{0:T(1024)S(1)} %bitcast.65, s32[2048]{0:T(1024)S(1)} %fusion.71), kind=kCustom, calls=%fused_computation.1 | custom fusion | bytes 24576 | tf_op jit(solution)/shard_map/gather | solution.py:123
  152.0 2.5 %collective-permute-start.21 = (f32[130,1]{1,0:T(8,128)S(1)}, f32[130,1]{1,0:T(8,128)S(1)}, u32[]{:S(2)}, u32[]{:S(2)}) collective-permute-start(f32[130,1]{1,0:T(8,128)S(1)} %get-tuple-element.17), channel_id=1, source_target_pairs={{0,1},{1,2},{2,3},{4,5},{5,6},{6,7},{8,9},{9,10},{10,11},{12,13},{... | collective-permute-start | bytes 1568 | tf_op jit(solution)/shard_map/ppermute | solution.py:39
  154.5 1.5 collective-permute-start.22
  156.1 11.8 %gather_fusion.2 = f32[2048]{0:T(1024)S(1)} fusion(f32[65536]{0:T(1024)S(1)} %bitcast.63, s32[2048]{0:T(1024)S(1)} %fusion.71), kind=kCustom, calls=%fused_computation.2 | custom fusion | bytes 24576 | tf_op jit(solution)/shard_map/gather | solution.py:124
  168.0 1.3 fusion.20
  170.1 11.8 %gather_fusion = f32[2048]{0:T(1024)S(1)} fusion(f32[65536]{0:T(1024)S(1)} %bitcast.64, s32[2048]{0:T(1024)S(1)} %fusion.71), kind=kCustom, calls=%fused_computation | custom fusion | bytes 24576 | tf_op jit(solution)/shard_map/gather | solution.py:123
  181.9 1.3 copy.20
  183.3 6.7 %scatter_custom_fusion = f32[3,6144]{0,1:T(8,128)S(1)} fusion(s32[2048]{0:T(1024)} %bitcast.77, f32[2048,3]{1,0:T(8,128)} %copy.20, f32[]{:T(128)} %constant.24.clone.1), kind=kCustom, calls=%fused_computation.34 | custom fusion | bytes 74240 | tf_op jit(solution)/shard_map/scatter | solution.py:129
  190.0 1.5 copy.21
  191.5 16.3 %all_to_all.9 = f32[3,32,192]{2,0,1:T(4,128)S(1)} all-to-all(f32[3,32,192]{2,0,1:T(4,128)S(1)} %copy.21), channel_id=1, replica_groups=mesh['gx'=8,'gy'=4] {'gx','gy'}, dimensions={1} | all-to-all | bytes 147456 | tf_op jit(solution)/shard_map/all_to_all | solution.py:130
  (110 shorter events, 29.1 us)
Async XLA Ops:
  1.9 26.7 %collective-permute-start = (f32[8,1,2048]{2,1,0:T(1,128)S(1)}, f32[8,1,2048]{2,1,0:T(1,128)S(1)}, u32[]{:S(2)}, u32[]{:S(2)}) collective-permute-start(f32[8,1,2048]{2,1,0:T(1,128)S(1)} %get-tuple-element.16), channel_id=1, source_target_pairs={{1,0},{2,1},{3,2},{4,3},{5,4},{6,5},{7,6},{8,7},{9,8},{10,9},{11,1... | collective-permute-start | bytes 196616 | tf_op jit(solution)/shard_map/ppermute | solution.py:40
  3.2 25.4 %collective-permute-start.1 = (f32[8,1,2048]{2,1,0:T(1,128)S(1)}, f32[8,1,2048]{2,1,0:T(1,128)S(1)}, u32[]{:S(2)}, u32[]{:S(2)}) collective-permute-start(f32[8,1,2048]{2,1,0:T(1,128)S(1)} %get-tuple-element.15), channel_id=1, source_target_pairs={{0,1},{1,2},{2,3},{3,4},{4,5},{5,6},{6,7},{7,8},{8,9},{9,10},{10,1... | collective-permute-start | bytes 196616 | tf_op jit(solution)/shard_map/ppermute | solution.py:39
  9.6 42.6 %collective-permute-start.7 = (f32[1,512]{1,0:T(1,128)S(1)}, f32[1,512]{1,0:T(1,128)S(1)}, u32[]{:S(2)}, u32[]{:S(2)}) collective-permute-start(f32[1,512]{1,0:T(1,128)S(1)} %get-tuple-element.30), channel_id=1, source_target_pairs={{0,4},{4,8},{8,12},{12,16},{16,20},{20,24},{24,28},{1,5},{5,9},{9,... | collective-permute-start | bytes 6152 | tf_op jit(solution)/shard_map/ppermute | solution.py:39
  13.6 39.8 %collective-permute-start.9 = (f32[1,512]{1,0:T(1,128)S(1)}, f32[1,512]{1,0:T(1,128)S(1)}, u32[]{:S(2)}, u32[]{:S(2)}) collective-permute-start(f32[1,512]{1,0:T(1,128)S(1)} %get-tuple-element.29), channel_id=1, source_target_pairs={{4,0},{8,4},{12,8},{16,12},{20,16},{24,20},{28,24},{5,1},{9,5},{13... | collective-permute-start | bytes 6152 | tf_op jit(solution)/shard_map/ppermute | solution.py:40
  32.8 6.3 %collective-permute-start.2 = (f32[8,1,2048]{2,1,0:T(1,128)S(1)}, f32[8,1,2048]{2,1,0:T(1,128)S(1)}, u32[]{:S(2)}, u32[]{:S(2)}) collective-permute-start(f32[8,1,2048]{2,1,0:T(1,128)S(1)} %get-tuple-element.14), channel_id=1, source_target_pairs={{1,0},{2,1},{3,2},{4,3},{5,4},{6,5},{7,6},{8,7},{9,8},{10,9},{11,1... | collective-permute-start | bytes 196616 | tf_op jit(solution)/shard_map/ppermute | solution.py:40
  34.1 6.7 %collective-permute-start.3 = (f32[8,1,2048]{2,1,0:T(1,128)S(1)}, f32[8,1,2048]{2,1,0:T(1,128)S(1)}, u32[]{:S(2)}, u32[]{:S(2)}) collective-permute-start(f32[8,1,2048]{2,1,0:T(1,128)S(1)} %get-tuple-element.13), channel_id=1, source_target_pairs={{0,1},{1,2},{2,3},{3,4},{4,5},{5,6},{6,7},{7,8},{8,9},{9,10},{10,1... | collective-permute-start | bytes 196616 | tf_op jit(solution)/shard_map/ppermute | solution.py:39
  44.0 15.2 %copy-start.3 = (f32[128,512]{1,0:T(8,128)S(1)}, f32[128,512]{1,0:T(8,128)}, u32[]{:S(2)}) copy-start(f32[128,512]{1,0:T(8,128)} %param.16) | copy-start | bytes 786436
  45.2 22.0 %collective-permute-start.4 = (f32[8,32,512]{2,1,0:T(8,128)}, f32[8,32,512]{2,1,0:T(8,128)}, u32[]{:S(2)}, u32[]{:S(2)}) collective-permute-start(f32[8,32,512]{2,1,0:T(8,128)} %get-tuple-element.11), channel_id=1, source_target_pairs={{0,1},{1,0},{2,3},{3,2},{4,5},{5,4},{6,7},{7,6},{8,9},{9,8},{10,11... | collective-permute-start | bytes 1572872 | tf_op jit(solution)/shard_map/ppermute | solution.py:27
  47.7 22.1 %collective-permute-start.5 = (f32[8,32,512]{2,1,0:T(8,128)}, f32[8,32,512]{2,1,0:T(8,128)}, u32[]{:S(2)}, u32[]{:S(2)}) collective-permute-start(f32[8,32,512]{2,1,0:T(8,128)} %get-tuple-element.10), channel_id=1, source_target_pairs={{0,2},{1,3},{2,0},{3,1},{4,6},{5,7},{6,4},{7,5},{8,10},{9,11},{10,... | collective-permute-start | bytes 1572872 | tf_op jit(solution)/shard_map/ppermute | solution.py:27
  51.4 33.7 %collective-permute-start.6 = (f32[8,32,512]{2,1,0:T(8,128)}, f32[8,32,512]{2,1,0:T(8,128)S(1)}, u32[]{:S(2)}, u32[]{:S(2)}) collective-permute-start(f32[8,32,512]{2,1,0:T(8,128)} %get-tuple-element.9), channel_id=1, source_target_pairs={{0,3},{1,2},{2,1},{3,0},{4,7},{5,6},{6,5},{7,4},{8,11},{9,10},{10,... | collective-permute-start | bytes 1572872 | tf_op jit(solution)/shard_map/ppermute | solution.py:27
  52.1 72.7 %copy-start.9 = (f32[1,512]{1,0:T(1,128)}, f32[1,512]{1,0:T(1,128)S(1)}, u32[]{:S(2)}) copy-start(f32[1,512]{1,0:T(1,128)S(1)} %collective-permute-done.7) | copy-start | bytes 6148
  52.1 7.1 %collective-permute-start.10 = (f32[1,512]{1,0:T(1,128)S(1)}, f32[1,512]{1,0:T(1,128)S(1)}, u32[]{:S(2)}, u32[]{:S(2)}) collective-permute-start(f32[1,512]{1,0:T(1,128)S(1)} %get-tuple-element.32), channel_id=1, source_target_pairs={{4,0},{8,4},{12,8},{16,12},{20,16},{24,20},{28,24},{5,1},{9,5},{13... | collective-permute-start | bytes 6152 | tf_op jit(solution)/shard_map/ppermute | solution.py:40
  53.4 71.4 %copy-start.11 = (f32[1,512]{1,0:T(1,128)}, f32[1,512]{1,0:T(1,128)S(1)}, u32[]{:S(2)}) copy-start(f32[1,512]{1,0:T(1,128)S(1)} %collective-permute-done.9) | copy-start | bytes 6148
  53.5 7.1 %collective-permute-start.8 = (f32[1,512]{1,0:T(1,128)S(1)}, f32[1,512]{1,0:T(1,128)S(1)}, u32[]{:S(2)}, u32[]{:S(2)}) collective-permute-start(f32[1,512]{1,0:T(1,128)S(1)} %get-tuple-element.31), channel_id=1, source_target_pairs={{0,4},{4,8},{8,12},{12,16},{16,20},{20,24},{24,28},{1,5},{5,9},{9,... | collective-permute-start | bytes 6152 | tf_op jit(solution)/shard_map/ppermute | solution.py:39
  59.2 25.9 %collective-permute-start.11 = (f32[130,1]{1,0:T(8,128)S(1)}, f32[130,1]{1,0:T(8,128)S(1)}, u32[]{:S(2)}, u32[]{:S(2)}) collective-permute-start(f32[130,1]{1,0:T(8,128)S(1)} %get-tuple-element.22), channel_id=1, source_target_pairs={{0,1},{1,2},{2,3},{4,5},{5,6},{6,7},{8,9},{9,10},{10,11},{12,13},{... | collective-permute-start | bytes 1568 | tf_op jit(solution)/shard_map/ppermute | solution.py:39
  60.5 24.6 %collective-permute-start.13 = (f32[130,1]{1,0:T(8,128)S(1)}, f32[130,1]{1,0:T(8,128)S(1)}, u32[]{:S(2)}, u32[]{:S(2)}) collective-permute-start(f32[130,1]{1,0:T(8,128)S(1)} %get-tuple-element.21), channel_id=1, source_target_pairs={{1,0},{2,1},{3,2},{5,4},{6,5},{7,6},{9,8},{10,9},{11,10},{13,12},{... | collective-permute-start | bytes 1568 | tf_op jit(solution)/shard_map/ppermute | solution.py:40
  67.2 17.9 %collective-permute-start.12 = (f32[130,1]{1,0:T(8,128)S(1)}, f32[130,1]{1,0:T(8,128)S(1)}, u32[]{:S(2)}, u32[]{:S(2)}) collective-permute-start(f32[130,1]{1,0:T(8,128)S(1)} %get-tuple-element.23), channel_id=1, source_target_pairs={{0,1},{1,2},{2,3},{4,5},{5,6},{6,7},{8,9},{9,10},{10,11},{12,13},{... | collective-permute-start | bytes 1568 | tf_op jit(solution)/shard_map/ppermute | solution.py:39
  69.8 18.8 %collective-permute-start.14 = (f32[130,1]{1,0:T(8,128)S(1)}, f32[130,1]{1,0:T(8,128)S(1)}, u32[]{:S(2)}, u32[]{:S(2)}) collective-permute-start(f32[130,1]{1,0:T(8,128)S(1)} %get-tuple-element.24), channel_id=1, source_target_pairs={{1,0},{2,1},{3,2},{5,4},{6,5},{7,6},{9,8},{10,9},{11,10},{13,12},{... | collective-permute-start | bytes 1568 | tf_op jit(solution)/shard_map/ppermute | solution.py:40
  88.6 42.0 %copy-start.15 = (s32[2048]{0:T(1024)S(1)}, s32[2048]{0:T(1024)}, u32[]{:S(2)}) copy-start(s32[2048]{0:T(1024)} %param.18) | copy-start | bytes 24580
  94.0 7.9 %collective-permute-start.15 = (f32[1,512]{1,0:T(1,128)S(1)}, f32[1,512]{1,0:T(1,128)S(1)}, u32[]{:S(2)}, u32[]{:S(2)}) collective-permute-start(f32[1,512]{1,0:T(1,128)S(1)} %get-tuple-element.27), channel_id=1, source_target_pairs={{0,4},{4,8},{8,12},{12,16},{16,20},{20,24},{24,28},{1,5},{5,9},{9,... | collective-permute-start | bytes 6152 | tf_op jit(solution)/shard_map/ppermute | solution.py:39
  100.6 8.4 %collective-permute-start.16 = (f32[1,512]{1,0:T(1,128)S(1)}, f32[1,512]{1,0:T(1,128)S(1)}, u32[]{:S(2)}, u32[]{:S(2)}) collective-permute-start(f32[1,512]{1,0:T(1,128)S(1)} %get-tuple-element.28), channel_id=1, source_target_pairs={{4,0},{8,4},{12,8},{16,12},{20,16},{24,20},{28,24},{5,1},{9,5},{13... | collective-permute-start | bytes 6152 | tf_op jit(solution)/shard_map/ppermute | solution.py:40
  109.1 11.4 %collective-permute-start.17 = (f32[130,1]{1,0:T(8,128)S(1)}, f32[130,1]{1,0:T(8,128)S(1)}, u32[]{:S(2)}, u32[]{:S(2)}) collective-permute-start(f32[130,1]{1,0:T(8,128)S(1)} %get-tuple-element.19), channel_id=1, source_target_pairs={{0,1},{1,2},{2,3},{4,5},{5,6},{6,7},{8,9},{9,10},{10,11},{12,13},{... | collective-permute-start | bytes 1568 | tf_op jit(solution)/shard_map/ppermute | solution.py:39
  118.6 6.2 %collective-permute-start.18 = (f32[130,1]{1,0:T(8,128)S(1)}, f32[130,1]{1,0:T(8,128)S(1)}, u32[]{:S(2)}, u32[]{:S(2)}) collective-permute-start(f32[130,1]{1,0:T(8,128)S(1)} %get-tuple-element.20), channel_id=1, source_target_pairs={{1,0},{2,1},{3,2},{5,4},{6,5},{7,6},{9,8},{10,9},{11,10},{13,12},{... | collective-permute-start | bytes 1568 | tf_op jit(solution)/shard_map/ppermute | solution.py:40
  125.9 25.4 %collective-permute-start.19 = (f32[1,512]{1,0:T(1,128)}, f32[1,512]{1,0:T(1,128)}, u32[]{:S(2)}, u32[]{:S(2)}) collective-permute-start(f32[1,512]{1,0:T(1,128)} %get-tuple-element.25), channel_id=1, source_target_pairs={{0,4},{4,8},{8,12},{12,16},{16,20},{20,24},{24,28},{1,5},{5,9},{9,... | collective-permute-start | bytes 6152 | tf_op jit(solution)/shard_map/ppermute | solution.py:39
  129.3 22.0 %collective-permute-start.20 = (f32[1,512]{1,0:T(1,128)}, f32[1,512]{1,0:T(1,128)}, u32[]{:S(2)}, u32[]{:S(2)}) collective-permute-start(f32[1,512]{1,0:T(1,128)} %get-tuple-element.26), channel_id=1, source_target_pairs={{4,0},{8,4},{12,8},{16,12},{20,16},{24,20},{28,24},{5,1},{9,5},{13... | collective-permute-start | bytes 6152 | tf_op jit(solution)/shard_map/ppermute | solution.py:40
  152.0 15.9 %collective-permute-start.21 = (f32[130,1]{1,0:T(8,128)S(1)}, f32[130,1]{1,0:T(8,128)S(1)}, u32[]{:S(2)}, u32[]{:S(2)}) collective-permute-start(f32[130,1]{1,0:T(8,128)S(1)} %get-tuple-element.17), channel_id=1, source_target_pairs={{0,1},{1,2},{2,3},{4,5},{5,6},{6,7},{8,9},{9,10},{10,11},{12,13},{... | collective-permute-start | bytes 1568 | tf_op jit(solution)/shard_map/ppermute | solution.py:39
  154.5 13.4 %collective-permute-start.22 = (f32[130,1]{1,0:T(8,128)S(1)}, f32[130,1]{1,0:T(8,128)}, u32[]{:S(2)}, u32[]{:S(2)}) collective-permute-start(f32[130,1]{1,0:T(8,128)S(1)} %get-tuple-element.18), channel_id=1, source_target_pairs={{1,0},{2,1},{3,2},{5,4},{6,5},{7,6},{9,8},{10,9},{11,10},{13,12},{... | collective-permute-start | bytes 1568 | tf_op jit(solution)/shard_map/ppermute | solution.py:40
  156.1 11.8 %copy-start.10 = (f32[1,512]{1,0:T(1,128)S(1)}, f32[1,512]{1,0:T(1,128)}, u32[]{:S(2)}) copy-start(f32[1,512]{1,0:T(1,128)} %copy-done.9) | copy-start | bytes 6148
  156.1 11.8 %copy-start.12 = (f32[1,512]{1,0:T(1,128)S(1)}, f32[1,512]{1,0:T(1,128)}, u32[]{:S(2)}) copy-start(f32[1,512]{1,0:T(1,128)} %copy-done.11) | copy-start | bytes 6148
  170.0 11.8 %copy-start.13 = (f32[2048]{0:T(1024)S(1)}, f32[2048]{0:T(1024)}, u32[]{:S(2)}) copy-start(f32[2048]{0:T(1024)} %gather_fusion.1) | copy-start | bytes 24580
  190.0 18.6 %copy-start.6 = (f32[2,1,6144]{2,1,0:T(1,128)S(1)}, f32[2,1,6144]{2,1,0:T(1,128)}, u32[]{:S(2)}) copy-start(f32[2,1,6144]{2,1,0:T(1,128)} %param.20) | copy-start | bytes 147460
  190.0 18.6 %copy-start.14 = (f32[1,6144]{1,0:T(1,128)S(1)}, f32[1,6144]{1,0:T(1,128)}, u32[]{:S(2)}) copy-start(f32[1,6144]{1,0:T(1,128)} %param.21) | copy-start | bytes 73732
  (9 other events, 40.7 us)
